TPU v7x, 256 devices: a whole 4x4x8 slice. The times are simulated.
256 devices in a mesh: dp: 32 (over x, z), mp: 8 (over y, core).
Axes of the slice: x: 4, y: 4, z: 8, core: 2. Of those that a mesh axis runs over, the one named last changes fastest.
Arguments:
- tokens: bfloat16 [8192, 8192], P(('dp', 'mp')), may hold values from -6 to 6
- upstream: bfloat16 [8192, 2, 28672], P(('dp', 'mp')), may hold values from -0.0625 to 0.0625
- deltas: bfloat16 [1024, 128, 128], P('mp'), may hold values from -0.5 to 0.5
- block_row: int32 [1024], P('mp'), may hold values from 0 to 63, as said below
- block_column: int32 [1024], P('mp'), may hold values from 0 to 55, as said below
- block_owner: int32 [1024], P('mp'), may hold values from 0 to 31, as said below
- block_count: int32 [8], P('mp'), may hold values from 64 to 128, as said below
Outputs:
- branch_out: bfloat16 [8192, 2, 28672], P('dp', None, 'mp')
- block_grads: float32 [8, 192, 128, 128], P('mp', 'dp')
Inputs may be any that keep to these rules, and one draw needn't show every extreme that they name: `block_row`: row tile of each slot's delta tile. `block_column`: column tile within the shard's gate columns (below 28) followed by its up columns; the tiles of one shard's slots are distinct. `block_owner`: among the live slots of one shard no dp index owns more than 6 tiles, and in every shard one dp index owns exactly 6. The live slots of a shard are its first block_count slots; some shard has all 128 live.
All inputs are finite; a program needn't handle non-finite values.
Results may differ from a plain program's by a relative error of at most 0.001.
Values may be sent and summed in bfloat16 or wider, within the bound.
No kernel may reach another device: no remote copies, remote signals or barrier semaphores. Data moves between devices by JAX's collectives and lax.ppermute only.
A program may use at most 128 MiB of HBM per device.

v0:
```python
import jax
import jax.numpy as jnp
from jax import lax
from jax.sharding import PartitionSpec as P


def pick_tiles(source, chosen):
    slot_ids = jnp.arange(chosen.shape[1], dtype=jnp.int32)
    source_index = jnp.sum(jnp.where(chosen, slot_ids[None, :], 0), axis=1)
    present = jnp.any(chosen, axis=1).astype(jnp.float32)
    return jnp.take(source, source_index, axis=0) * present[:, None, None]


def local(tokens, upstream, deltas, block_row, block_column, block_owner, block_count):
    model_width = tokens.shape[1]
    tile_size = deltas.shape[1]
    slot_count = deltas.shape[0]
    hidden = lax.all_to_all(upstream, "mp", split_axis=2, concat_axis=0, tiled=True)
    group_rows = hidden.shape[0]
    column_blocks = hidden.shape[1] * hidden.shape[2] // tile_size
    hidden_major = jnp.transpose(hidden.reshape(group_rows, column_blocks, tile_size), (1, 0, 2))
    upstream_chosen = jnp.take(hidden_major, block_column, axis=0)
    slot_ids = jnp.arange(slot_count, dtype=jnp.int32)
    live_slots = slot_ids < block_count[0]
    column_table = (
        live_slots[:, None]
        & (block_column[:, None] == jnp.arange(column_blocks, dtype=jnp.int32)[None, :])
    ).astype(jnp.float32)
    shard_rows = lax.all_gather(tokens, "mp", axis=0, tiled=True)
    row_count = shard_rows.shape[0]
    row_major = jnp.transpose(
        shard_rows.reshape(row_count, model_width // tile_size, tile_size), (1, 0, 2)
    )
    feature_tiles = jnp.take(row_major, block_row, axis=0)
    product = jnp.einsum("kni,kio->kno", feature_tiles, deltas, preferred_element_type=jnp.float32)
    rows_out = jnp.einsum("kc,kno->cno", column_table, product, precision=lax.Precision.HIGHEST)
    placed = rows_out
    grad_sum = jnp.einsum(
        "kni,kno->kio", feature_tiles, upstream_chosen, preferred_element_type=jnp.float32
    )
    placed, grad_sum = (placed, grad_sum)
    branch_out = jnp.transpose(placed.astype(jnp.bfloat16), (1, 0, 2)).reshape(
        group_rows, hidden.shape[1], hidden.shape[2]
    )
    dp_count = lax.axis_size("dp")
    owner_cap = 3 * slot_count // (2 * dp_count)
    owner_hot = (
        (block_owner[:, None] == jnp.arange(dp_count, dtype=jnp.int32)[None, :])
        & live_slots[:, None]
    ).astype(jnp.int32)
    before = jnp.cumsum(owner_hot, axis=0) - owner_hot
    owner_rank = jnp.sum(before * owner_hot, axis=1)
    summed = lax.psum(grad_sum, "dp")
    my_owner = lax.axis_index("dp")
    chosen = (
        live_slots[None, :]
        & (block_owner[None, :] == my_owner)
        & (owner_rank[None, :] == jnp.arange(owner_cap, dtype=jnp.int32)[:, None])
    )
    owned = pick_tiles(summed, chosen)
    return (branch_out, owned[None])


def solution(mesh):
    placed = (
        P(("dp", "mp"), None),
        P(("dp", "mp"), None, None),
        P("mp", None, None),
        P("mp"),
        P("mp"),
        P("mp"),
        P("mp"),
    )
    return jax.shard_map(
        local,
        mesh=mesh,
        in_specs=placed,
        out_specs=(P("dp", None, "mp"), P("mp", "dp", None, None)),
        check_vma=False,
    )
```

profile of v0, /device:TPU:1, one launch (start us, length us, event | category | flops | bytes accessed | tf_op | source)
XLA Modules:
  0.0 435.7 jit_solution(1149873122995598057)
XLA Ops:
  7.2 0.0 all-gather.2.cloned.1.call-start
  7.2 0.7 all-gather.2.cloned.1.call-update
  7.9 34.9 %copy.36 = bf16[32,2,28672]{0,1,2:T(2,128)(2,1)} copy(bf16[32,2,28672]{2,1,0:T(2,128)(2,1)} %param.8) | data formatting | bytes 7340032 | tf_op args[1]
  42.8 0.0 copy-start.2
  42.8 0.0 copy-start.1
  42.8 16.5 %reshape.95 = bf16[8,2,114688]{2,1,0:T(2,128)(2,1)} reshape(bf16[28672,2,32]{2,1,0:T(2,128)(2,1)} %bitcast.26) | data formatting | bytes 7340032
  59.4 7.6 %all-to-all-start = ((bf16[8,2,114688]{2,1,0:T(2,128)(2,1)}), bf16[8,2,114688]{2,1,0:T(2,128)(2,1)}, u32[]{:S(2)}, u32[]{:S(2)}) async-start(bf16[8,2,114688]{2,1,0:T(2,128)(2,1)} %reshape.95), calls=%async_computation | async-start | bytes 7340032 | tf_op jit(solution)/shard_map/all_to_all | solution.py:18
  66.9 0.0 all-reduce.2.cloned.1.call-start
  66.9 0.0 copy-done.2
  67.0 0.0 copy-done.1
  67.0 43.1 %all-to-all-done = bf16[8,2,114688]{2,1,0:T(2,128)(2,1)} async-done(((bf16[8,2,114688]{2,1,0:T(2,128)(2,1)}), bf16[8,2,114688]{2,1,0:T(2,128)(2,1)}, u32[]{:S(2)}, u32[]{:S(2)}) %all-to-all-start) | async-done | bytes 3670048 | tf_op jit(solution)/shard_map/all_to_all | solution.py:18
  110.1 11.6 %reshape.96 = bf16[28672,2,32]{2,1,0:T(2,128)(2,1)} reshape(bf16[8,2,114688]{2,1,0:T(2,128)(2,1)} %all-to-all-done) | data formatting | bytes 7340032
  121.7 35.0 %copy.37 = bf16[32,2,8,3584]{3,1,0,2:T(2,128)(2,1)} copy(bf16[32,2,8,3584]{0,1,3,2:T(2,128)(2,1)} %bitcast.25) | data formatting | bytes 7340032 | tf_op jit(solution)/shard_map/all_to_all | solution.py:18
  156.8 9.2 %reshape.67 = bf16[256,56,128]{2,1,0:T(8,128)(2,1)} reshape(bf16[8,32,2,3584]{3,2,1,0:T(2,128)(2,1)} %bitcast.30) | data formatting | bytes 7340032 | tf_op jit(solution)/shard_map/reshape | solution.py:21
  165.9 4.8 %copy.46 = bf16[256,56,128]{2,0,1:T(8,128)(2,1)} copy(bf16[256,56,128]{2,1,0:T(8,128)(2,1)} %reshape.67) | data formatting | bytes 7340032 | tf_op jit(solution)/shard_map/reshape | solution.py:21
  170.7 8.6 %gather_fusion.1 = bf16[128,256,128]{2,1,0:T(8,128)(2,1)} fusion(bf16[56,256,128]{2,1,0:T(8,128)(2,1)} %bitcast.27, s32[1024]{0:T(1024)S(1)} %pad_clamp_fusion.1), kind=kCustom, calls=%fused_computation.1 | custom fusion | bytes 16777728 | tf_op jit(solution)/shard_map/jit(_take)/gather | solution.py:22
  179.3 0.0 all-gather.2.cloned.1.call-done
  179.3 6.4 %copy.33 = bf16[256,8192]{0,1:T(8,128)(2,1)} copy(bf16[256,8192]{1,0:T(8,128)(2,1)} %all-gather.2.cloned.1.call-done) | data formatting | bytes 8388608 | tf_op jit(solution)/shard_map/all_gather | solution.py:29
  185.7 6.4 %copy.34 = bf16[256,64,128]{2,0,1:T(8,128)(2,1)} copy(bf16[256,64,128]{0,2,1:T(8,128)(2,1)} %bitcast.29) | data formatting | bytes 8388608 | tf_op jit(solution)/shard_map/reshape | solution.py:32
  192.1 8.7 %gather_fusion = bf16[128,256,128]{2,1,0:T(8,128)(2,1)} fusion(bf16[64,256,128]{2,1,0:T(8,128)(2,1)} %bitcast.28, s32[1024]{0:T(1024)S(1)} %pad_clamp_fusion.2), kind=kCustom, calls=%fused_computation | custom fusion | bytes 16777728 | tf_op jit(solution)/shard_map/jit(_take)/gather | solution.py:34
  200.8 11.9 %fusion.2 = f32[128,128,128]{2,1,0:T(8,128)} fusion(bf16[128,256,128]{2,1,0:T(8,128)(2,1)} %gather_fusion.1, pred[128]{0:T(512)(128)(4,1)S(1)} %get-tuple-element.4, bf16[128,256,128]{2,1,0:T(8,128)(2,1)} %gather_fusion, pred[128]{0:T(512)(128)(4,1)S(1)} %get-tuple-element.5), kind=kOutput, calls=%fused_computation.5 | convolution fusion | flops 1082130432 | bytes 25166080 | tf_op jit(solution)/shard_map/kni,kno->kio/dot_general | solution.py:38
  212.7 0.0 copy-start
  212.7 0.0 all-reduce.2.cloned.1.call-update
  213.4 0.0 copy-done
  213.4 0.1 fusion.11
  213.5 0.2 reduce_window_sum.11
  213.7 0.2 select_reduce_fusion
  213.9 0.1 fusion.18
  214.0 0.1 select_reduce_fusion.1
  214.2 13.5 %fusion.6 = f32[128,256,128]{2,1,0:T(8,128)} fusion(bf16[128,128,128]{2,1,0:T(8,128)(2,1)} %param.9, bf16[128,256,128]{2,1,0:T(8,128)(2,1)} %gather_fusion, pred[128]{0:T(512)(128)(4,1)S(1)} %get-tuple-element.5), kind=kOutput, calls=%fused_computation.12 | convolution fusion | flops 1077936128 | bytes 29360256 | tf_op jit(solution)/shard_map/kni,kio->kno/dot_general | solution.py:35
  227.7 22.6 %convert_bitcast_fusion = bf16[256,56,128]{2,1,0:T(8,128)(2,1)} fusion(f32[128,256,128]{2,1,0:T(8,128)} %fusion.6, s32[128]{0:T(128)S(1)} %copy-done.1, pred[128]{0:T(512)(128)(4,1)S(1)} %get-tuple-element.3), kind=kOutput, calls=%fused_computation.11 | convolution fusion | flops 2820421632 | bytes 20447872 | tf_op jit(solution)/shard_map/kc,kno->cno/dot_general | solution.py:36
  250.4 8.2 %reshape.66 = bf16[256,2,3584]{2,1,0:T(2,128)(2,1)} reshape(bf16[256,56,128]{2,1,0:T(8,128)(2,1)} %convert_bitcast_fusion) | data formatting | bytes 7340032 | tf_op jit(solution)/shard_map/reshape | solution.py:42
  258.5 165.6 %all-reduce.2.cloned.1.call-done = f32[128,128,128]{2,1,0:T(8,128)} async-done(((f32[128,128,128]{2,1,0:T(8,128)}), f32[128,128,128]{2,1,0:T(8,128)}) %all-reduce.2.cloned.1.call-update) | async-done | bytes 8388624 | tf_op jit(solution)/shard_map/psum | solution.py:53
  424.1 4.0 gather_fusion.2
  428.0 0.9 fusion.9
  (10 shorter events, 0.1 us)
Async XLA Ops:
  7.2 172.2 %all-gather.2.cloned.1.call-start = ((), (), s32[]{:S(2)}) async-start(), calls=%async_computation.1 | async-start | bytes 4718592 | tf_op jit(solution)/shard_map/all_gather | solution.py:29
  42.8 24.1 %copy-start.2 = (s32[128]{0:T(128)S(1)}, s32[128]{0:T(128)}, u32[]{:S(2)}) copy-start(s32[128]{0:T(128)} %param.10) | copy-start | bytes 1540
  42.8 24.1 %copy-start.1 = (s32[128]{0:T(128)S(1)}, s32[128]{0:T(128)}, u32[]{:S(2)}) copy-start(s32[128]{0:T(128)} %param.11) | copy-start | bytes 1540
  59.4 50.7 %all-to-all-start = ((bf16[8,2,114688]{2,1,0:T(2,128)(2,1)}), bf16[8,2,114688]{2,1,0:T(2,128)(2,1)}, u32[]{:S(2)}, u32[]{:S(2)}) async-start(bf16[8,2,114688]{2,1,0:T(2,128)(2,1)} %reshape.95), calls=%async_computation | async-start | bytes 7340032 | tf_op jit(solution)/shard_map/all_to_all | solution.py:18
  66.9 357.1 %all-reduce.2.cloned.1.call-start = ((), (), s32[]{:S(2)}) async-start(), calls=%async_computation.2 | async-start | bytes 16777216 | tf_op jit(solution)/shard_map/psum | solution.py:53
  212.7 0.7 copy-start
Sparse Core Ops, SparseCore 0:
  9.8 38.8 all-gather.1
  212.9 211.1 all-reduce.1
where the time goes:
time: 440 us; the launch traced here: 436 us
  waiting for transfers between devices  209 us (48%)
  local copies, waits for them, and re-layouts  154 us (35%)
  matrix products  48.1 us (11%)
  between operations  14.8 us (3%)
  starting transfers between devices  7.59 us (2%)
    psum x1, waiting for transfers between devices, local(): summed = lax.psum(grad_sum, 'dp')  166 us
    unnamed x9, local copies, waits for them, and re-layouts  63.1 us
    all_to_all x1, waiting for transfers between devices, local(): lax.all_to_all(upstream, 'mp', split_axis=2, concat_axis=0, tiled=True)  43.1 us
    all_to_all x1, local copies, waits for them, and re-layouts, local(): lax.all_to_all(upstream, 'mp', split_axis=2, concat_axis=0, tiled=True)  35 us
    dot_general x1, matrix products, local(): jnp.einsum('kc,kno->cno', column_table, product, precision=lax.Precision....  22.6 us
    reshape x2, local copies, waits for them, and re-layouts, local(): hidden.reshape(group_rows, column_blocks, tile_size)  14 us
    dot_general x1, matrix products, local(): jnp.einsum('kni,kio->kno', feature_tiles, deltas, preferred_element_type=...  13.5 us
    dot_general x1, matrix products, local(): jnp.einsum('kni,kno->kio', feature_tiles, upstream_chosen, preferred_elem...  11.9 us
  transfers between devices with their start and end apart: 3, of which 2 were waited for; matrix products, arithmetic and copies ran while one was open for 38% of the time, Pallas kernels for 0%

commit v1 on v0

--- a/solution.py
+++ b/solution.py
@@ -15,7 +15,10 @@
     model_width = tokens.shape[1]
     tile_size = deltas.shape[1]
     slot_count = deltas.shape[0]
-    hidden = lax.all_to_all(upstream, "mp", split_axis=2, concat_axis=0, tiled=True)
+    hidden = jnp.concatenate(
+        lax.all_to_all(jnp.stack(jnp.split(upstream, lax.axis_size("mp"), axis=2)), "mp", 0, 0),
+        axis=0,
+    )
     group_rows = hidden.shape[0]
     column_blocks = hidden.shape[1] * hidden.shape[2] // tile_size
     hidden_major = jnp.transpose(hidden.reshape(group_rows, column_blocks, tile_size), (1, 0, 2))

time: 440 us -> 367 us (0.83)
  local copies, waits for them, and re-layouts: 154 us -> 72.9 us
  waiting for transfers between devices: 209 us -> 220 us
    unnamed x9 -> x13, local copies, waits for them, and re-layouts: 63.1 us -> 14.7 us
    all_to_all x1 -> x0, local copies, waits for them, and re-layouts: 35 us -> none  [local(): lax.all_to_all(upstream, 'mp', split_axis=2, concat_axis=0, tiled=True)]
    another operation x0 -> x3, local copies, waits for them, and re-layouts: none -> 16.1 us  [the longest x2 13.9 us: local(): hidden.reshape(group_rows, column_blocks, tile_size)]
    reshape x2 -> x0, local copies, waits for them, and re-layouts: 14 us -> none  [local(): hidden.reshape(group_rows, column_blocks, tile_size)]
    all_to_all x1, waiting for transfers between devices: 43.1 us -> 54.1 us  [local(): lax.all_to_all(jnp.stack(jnp.split(upstream, lax.axis_size('mp'), axis=2)...]
  transfers between devices with their start and end apart: 3 -> 3, of which waited for: 2 -> 2; matrix products, arithmetic and copies ran while one was open for 38% -> 23% of each run, Pallas kernels for 0% -> 0%
where the time goes in v1:
time: 367 us; the launch traced here: 365 us
  waiting for transfers between devices  220 us (60%)
  local copies, waits for them, and re-layouts  72.9 us (20%)
  matrix products  48.1 us (13%)
  between operations  14.8 us (4%)
  starting transfers between devices  7.65 us (2%)
    psum x1, waiting for transfers between devices, local(): summed = lax.psum(grad_sum, 'dp')  166 us
    all_to_all x1, waiting for transfers between devices, local(): lax.all_to_all(jnp.stack(jnp.split(upstream, lax.axis_size('mp'), axis=2)...  54.1 us
    dot_general x1, matrix products, local(): jnp.einsum('kc,kno->cno', column_table, product, precision=lax.Precision....  22.6 us
    unnamed x13, local copies, waits for them, and re-layouts  14.7 us
    another operation x2, local copies, waits for them, and re-layouts, local(): hidden.reshape(group_rows, column_blocks, tile_size)  13.9 us
    dot_general x1, matrix products, local(): jnp.einsum('kni,kio->kno', feature_tiles, deltas, preferred_element_type=...  13.6 us
    dot_general x1, matrix products, local(): jnp.einsum('kni,kno->kio', feature_tiles, upstream_chosen, preferred_elem...  11.9 us
    gather x1, local copies, waits for them, and re-layouts, local(): feature_tiles = jnp.take(row_major, block_row, axis=0)  8.73 us
  transfers between devices with their start and end apart: 3, of which 2 were waited for; matrix products, arithmetic and copies ran while one was open for 23% of the time, Pallas kernels for 0%

profile of v1, /device:TPU:1, one launch (start us, length us, event | category | flops | bytes accessed | tf_op | source)
XLA Modules:
  0.0 365.4 jit_solution(15571713147260563371)
XLA Ops:
  7.2 0.0 all-gather.2.cloned.1.call-start
  7.2 0.7 all-gather.2.cloned.1.call-update
  7.9 2.1 bitcast_dynamic-update-slice_fusion.7
  10.0 2.1 bitcast_dynamic-update-slice_fusion.6
  12.1 2.1 bitcast_dynamic-update-slice_fusion.5
  14.2 2.1 bitcast_dynamic-update-slice_fusion.4
  16.3 2.1 bitcast_dynamic-update-slice_fusion.3
  18.4 2.1 bitcast_dynamic-update-slice_fusion.2
  20.5 2.1 bitcast_dynamic-update-slice_fusion.1
  22.6 0.0 copy-start.2
  22.6 0.0 copy-start.1
  22.6 2.1 bitcast_dynamic-update-slice_fusion
  24.7 7.6 %all-to-all-start = ((bf16[8,32,2,3584]{3,2,1,0:T(2,128)(2,1)}), bf16[8,32,2,3584]{3,2,1,0:T(2,128)(2,1)}, u32[]{:S(2)}, u32[]{:S(2)}) async-start(bf16[8,32,2,3584]{3,2,1,0:T(2,128)(2,1)} %bitcast_dynamic-update-slice_fusion), calls=%async_computation | async-start | bytes 7340032 | tf_op jit(solution)/shard_map/all_to_all | solution.py:19
  32.3 0.0 all-reduce.2.cloned.1.call-start
  32.3 0.0 copy-done.2
  32.4 0.0 copy-done.1
  32.4 54.1 %all-to-all-done = bf16[8,32,2,3584]{3,2,1,0:T(2,128)(2,1)} async-done(((bf16[8,32,2,3584]{3,2,1,0:T(2,128)(2,1)}), bf16[8,32,2,3584]{3,2,1,0:T(2,128)(2,1)}, u32[]{:S(2)}, u32[]{:S(2)}) %all-to-all-start) | async-done | bytes 3670048 | tf_op jit(solution)/shard_map/all_to_all | solution.py:19
  86.5 9.2 %reshape_reshape.3 = bf16[256,56,128]{2,1,0:T(8,128)(2,1)} reshape(bf16[8,32,2,3584]{3,2,1,0:T(2,128)(2,1)} %all-to-all-done) | data formatting | bytes 7340032 | tf_op jit(solution)/shard_map/reshape;reshape | solution.py:24
  95.7 4.8 %copy.32 = bf16[256,56,128]{2,0,1:T(8,128)(2,1)} copy(bf16[256,56,128]{2,1,0:T(8,128)(2,1)} %reshape_reshape.3) | data formatting | bytes 7340032 | tf_op jit(solution)/shard_map/reshape;reshape | solution.py:24
  100.4 8.6 %gather_fusion.1 = bf16[128,256,128]{2,1,0:T(8,128)(2,1)} fusion(bf16[56,256,128]{2,1,0:T(8,128)(2,1)} %bitcast.37, s32[1024]{0:T(1024)S(1)} %get-tuple-element.2), kind=kCustom, calls=%fused_computation.1 | custom fusion | bytes 16777728 | tf_op jit(solution)/shard_map/jit(_take)/gather | solution.py:25
  109.0 0.0 all-gather.2.cloned.1.call-done
  109.0 6.4 %copy.21 = bf16[256,8192]{0,1:T(8,128)(2,1)} copy(bf16[256,8192]{1,0:T(8,128)(2,1)} %all-gather.2.cloned.1.call-done) | data formatting | bytes 8388608 | tf_op jit(solution)/shard_map/all_gather | solution.py:32
  115.4 6.3 %copy.22 = bf16[256,64,128]{2,0,1:T(8,128)(2,1)} copy(bf16[256,64,128]{0,2,1:T(8,128)(2,1)} %bitcast.39) | data formatting | bytes 8388608 | tf_op jit(solution)/shard_map/reshape | solution.py:35
  121.7 8.7 %gather_fusion = bf16[128,256,128]{2,1,0:T(8,128)(2,1)} fusion(bf16[64,256,128]{2,1,0:T(8,128)(2,1)} %bitcast.38, s32[1024]{0:T(1024)S(1)} %get-tuple-element.3), kind=kCustom, calls=%fused_computation | custom fusion | bytes 16777728 | tf_op jit(solution)/shard_map/jit(_take)/gather | solution.py:37
  130.5 11.9 %fusion.2 = f32[128,128,128]{2,1,0:T(8,128)} fusion(bf16[128,256,128]{2,1,0:T(8,128)(2,1)} %gather_fusion.1, pred[128]{0:T(512)(128)(4,1)S(1)} %get-tuple-element.6, bf16[128,256,128]{2,1,0:T(8,128)(2,1)} %gather_fusion, pred[128]{0:T(512)(128)(4,1)S(1)} %get-tuple-element.7), kind=kOutput, calls=%fused_computation.5 | convolution fusion | flops 1082130432 | bytes 25166080 | tf_op jit(solution)/shard_map/kni,kno->kio/dot_general | solution.py:41
  142.4 0.0 copy-start
  142.4 0.0 all-reduce.2.cloned.1.call-update
  143.1 0.0 copy-done
  143.1 0.1 fusion.11
  143.2 0.2 reduce_window_sum.11
  143.4 0.2 select_reduce_fusion
  143.6 0.1 fusion.18
  143.7 0.1 select_reduce_fusion.1
  143.9 13.6 %fusion.6 = f32[128,256,128]{2,1,0:T(8,128)} fusion(bf16[128,128,128]{2,1,0:T(8,128)(2,1)} %param.9, bf16[128,256,128]{2,1,0:T(8,128)(2,1)} %gather_fusion, pred[128]{0:T(512)(128)(4,1)S(1)} %get-tuple-element.7), kind=kOutput, calls=%fused_computation.12 | convolution fusion | flops 1077936128 | bytes 29360256 | tf_op jit(solution)/shard_map/kni,kio->kno/dot_general | solution.py:38
  157.4 22.6 %convert_bitcast_fusion = bf16[256,56,128]{2,1,0:T(8,128)(2,1)} fusion(f32[128,256,128]{2,1,0:T(8,128)} %fusion.6, s32[128]{0:T(128)S(1)} %copy-done.1, pred[128]{0:T(512)(128)(4,1)S(1)} %get-tuple-element.5), kind=kOutput, calls=%fused_computation.11 | convolution fusion | flops 2820421632 | bytes 20447872 | tf_op jit(solution)/shard_map/kc,kno->cno/dot_general | solution.py:39
  180.1 8.2 %reshape.62 = bf16[256,2,3584]{2,1,0:T(2,128)(2,1)} reshape(bf16[256,56,128]{2,1,0:T(8,128)(2,1)} %convert_bitcast_fusion) | data formatting | bytes 7340032 | tf_op jit(solution)/shard_map/reshape | solution.py:45
  188.2 165.5 %all-reduce.2.cloned.1.call-done = f32[128,128,128]{2,1,0:T(8,128)} async-done(((f32[128,128,128]{2,1,0:T(8,128)}), f32[128,128,128]{2,1,0:T(8,128)}) %all-reduce.2.cloned.1.call-update) | async-done | bytes 8388624 | tf_op jit(solution)/shard_map/psum | solution.py:56
  353.8 4.0 %gather_fusion.2 = f32[6,128,128]{2,1,0:T(8,128)S(1)} fusion(f32[128,128,128]{2,1,0:T(8,128)} %all-reduce.2.cloned.1.call-done, s32[1024]{0:T(1024)S(1)} %pad_clamp_fusion), kind=kCustom, calls=%fused_computation.2 | custom fusion | bytes 786456 | tf_op jit(solution)/shard_map/jit(_take)/gather | solution.py:11
  357.7 0.9 fusion.9
  (9 shorter events, 0.1 us)
Async XLA Ops:
  7.2 101.9 %all-gather.2.cloned.1.call-start = ((), (), s32[]{:S(2)}) async-start(), calls=%async_computation.1 | async-start | bytes 4718592 | tf_op jit(solution)/shard_map/all_gather | solution.py:32
  22.6 9.7 %copy-start.2 = (s32[128]{0:T(128)S(1)}, s32[128]{0:T(128)}, u32[]{:S(2)}) copy-start(s32[128]{0:T(128)} %param.10) | copy-start | bytes 1540
  22.6 9.8 %copy-start.1 = (s32[128]{0:T(128)S(1)}, s32[128]{0:T(128)}, u32[]{:S(2)}) copy-start(s32[128]{0:T(128)} %param.11) | copy-start | bytes 1540
  24.7 61.7 %all-to-all-start = ((bf16[8,32,2,3584]{3,2,1,0:T(2,128)(2,1)}), bf16[8,32,2,3584]{3,2,1,0:T(2,128)(2,1)}, u32[]{:S(2)}, u32[]{:S(2)}) async-start(bf16[8,32,2,3584]{3,2,1,0:T(2,128)(2,1)} %bitcast_dynamic-update-slice_fusion), calls=%async_computation | async-start | bytes 7340032 | tf_op jit(solution)/shard_map/all_to_all | solution.py:19
  32.3 321.4 %all-reduce.2.cloned.1.call-start = ((), (), s32[]{:S(2)}) async-start(), calls=%async_computation.2 | async-start | bytes 16777216 | tf_op jit(solution)/shard_map/psum | solution.py:56
  142.4 0.7 copy-start
Sparse Core Ops, SparseCore 0:
  9.8 54.3 all-gather.1
  142.6 211.1 all-reduce.1
